TPU v7x, 32 devices: a whole 2x2x4 slice. The times are simulated.
32 devices in a mesh: grp: 8 (over y, x, core), ent: 4 (over z).
Axes of the slice: x: 2, y: 2, z: 4, core: 2. Of those that a mesh axis runs over, the one named last changes fastest.
Arguments:
- factor: bfloat16 [4096, 256], P(('grp', 'ent')), may hold values from -1.5 to 1.5
- cores: bfloat16 [16, 256, 256], replicated, may hold values from -0.375 to 0.375
- adjacency: int32 [768, 128, 128], P(('grp', 'ent')), may hold values 0 or 1
- tile_rels: int32 [32, 24], P(('grp', 'ent')), may hold values from 0 to 15
- tile_count: int32 [32], P(('grp', 'ent')), may hold values from 1 to 24, 480 in all
- send_lists: int32 [32, 4, 6], P(('grp', 'ent')), may hold values from 0 to 7
Outputs:
- factor_grad: float32 [4096, 256], P(('grp', 'ent'))
All inputs are finite; a program needn't handle non-finite values. No bound on the sum of `adjacency` or of `tile_count` on one device may be relied on, other than what follows from the above.
Results may differ from a plain program's by a relative error of at most 0.002.
Values may be sent and summed in bfloat16 or wider, within the bound.
No kernel may reach another device: no remote copies, remote signals or barrier semaphores. Data moves between devices by JAX's collectives and lax.ppermute only.
A program may use at most 64 MiB of HBM per device.

v0:
```python
import jax
import jax.numpy as jnp
from jax import lax
from jax.sharding import PartitionSpec as P

LOSS_SCALE = 0.0625


def on_device(factor, cores, adjacency, tile_rels, tile_count, send_lists):
    ent_count = lax.axis_size("ent")
    grp_count = lax.axis_size("grp")
    my_ent = lax.axis_index("ent")
    tiles = tile_rels.shape[1]
    block = factor.shape[0]
    width = factor.shape[1]
    per_relay = tiles // ent_count
    slots = ent_count * per_relay
    relations = tile_rels[0]
    routes = send_lists[0].reshape(slots)
    group_blocks = lax.all_gather(factor[None], "grp", axis=0, tiled=True)
    outgoing = group_blocks[routes].reshape(ent_count, per_relay, block, width)
    arrived = lax.all_to_all(outgoing, "ent", split_axis=0, concat_axis=0, tiled=True).reshape(
        slots, block, width
    )
    tile_ids = jnp.arange(tiles, dtype=jnp.int32)
    slot_of_tile = (my_ent + tile_ids) % ent_count * per_relay + tile_ids // ent_count
    factor_panels = arrived[slot_of_tile]
    live = (tile_ids < tile_count[0]).astype(jnp.float32)
    by_relation = jnp.einsum(
        "br,krs->kbs", factor, cores, preferred_element_type=jnp.float32
    ).astype(jnp.bfloat16)
    mapped_tiles = by_relation[relations]
    predicted_scores = jnp.einsum(
        "ogj,omj->ogm", mapped_tiles, factor_panels, preferred_element_type=jnp.float32
    )
    score_residual = (
        (predicted_scores - adjacency.astype(jnp.float32)) * (LOSS_SCALE * live)[:, None, None]
    ).astype(jnp.bfloat16)
    relation_product = jnp.einsum(
        "xmw,xwe->xme", score_residual, factor_panels, preferred_element_type=jnp.float32
    ).astype(jnp.bfloat16)
    row_grad = jnp.einsum(
        "tbs,trs->br", relation_product, cores[relations], preferred_element_type=jnp.float32
    )
    slot_ids = jnp.arange(slots, dtype=jnp.int32)
    tile_of_slot = slot_ids % per_relay * ent_count + (slot_ids // per_relay - my_ent) % ent_count
    column_terms = jnp.einsum(
        "yzj,yzh->yjh", score_residual, mapped_tiles, preferred_element_type=jnp.float32
    ).astype(jnp.bfloat16)
    sent_terms = column_terms[tile_of_slot].reshape(ent_count, per_relay, block, width)
    returned = (
        lax.all_to_all(sent_terms, "ent", split_axis=0, concat_axis=0, tiled=True)
        .reshape(slots, block * width)
        .astype(jnp.float32)
    )
    owner_onehot = (routes[:, None] == jnp.arange(grp_count, dtype=jnp.int32)[None, :]).astype(
        jnp.float32
    )
    owner_terms = jnp.dot(
        owner_onehot.T,
        returned,
        precision=lax.Precision.HIGHEST,
        preferred_element_type=jnp.float32,
    )
    owner_part = lax.psum_scatter(
        owner_terms.reshape(grp_count, block, width), "grp", scatter_dimension=0, tiled=True
    )
    return row_grad + owner_part[0]


def solution(mesh):
    in_specs = (
        P(("grp", "ent"), None),
        P(),
        P(("grp", "ent"), None, None),
        P(("grp", "ent"), None),
        P(("grp", "ent")),
        P(("grp", "ent"), None, None),
    )
    out_specs = P(("grp", "ent"), None)
    return jax.shard_map(
        on_device, mesh=mesh, in_specs=in_specs, out_specs=out_specs, check_vma=False
    )
```

profile of v0, /device:TPU:0, one launch (start us, length us, event | category | flops | bytes accessed | tf_op | source)
XLA Modules:
  0.0 166.0 jit_solution(857811333616795226)
XLA Ops:
  6.5 0.0 copy-start
  6.5 0.9 reshape_squeeze.3
  7.5 11.6 %all-gather = bf16[1024,256]{1,0:T(8,128)(2,1)S(1)} all-gather(bf16[128,256]{1,0:T(8,128)(2,1)} %param.6), channel_id=2, replica_groups=mesh['grp'=8,'ent'=4] {'grp'}, dimensions={0}, use_global_device_ids=true | all-gather | bytes 589824 | tf_op jit(solution)/shard_map/all_gather | solution.py:20
  19.1 1.9 %gather_fusion.1 = bf16[24,128,256]{2,1,0:T(8,128)(2,1)} fusion(bf16[8,128,256]{2,1,0:T(8,128)(2,1)S(1)} %bitcast.50, s32[1024]{0:T(1024)S(1)} %pad_clamp_fusion.2), kind=kCustom, calls=%fused_computation.1 | custom fusion | bytes 3145824 | tf_op jit(solution)/shard_map/gather | solution.py:21
  20.9 5.0 %all-to-all-start = ((bf16[4,6,128,256]{3,2,1,0:T(8,128)(2,1)}), bf16[4,6,128,256]{3,2,1,0:T(8,128)(2,1)}, u32[]{:S(2)}, u32[]{:S(2)}) async-start(bf16[4,6,128,256]{3,2,1,0:T(8,128)(2,1)} %bitcast.51), calls=%async_computation | async-start | bytes 3145728 | tf_op jit(solution)/shard_map/all_to_all | solution.py:22
  26.6 0.0 copy-done.4
  26.6 0.0 copy-done
  26.6 0.8 fusion.4
  27.4 1.9 %gather_fusion = bf16[24,128,256]{1,2,0:T(8,128)(2,1)} fusion(bf16[16,128,256]{1,2,0:T(8,128)(2,1)S(1)} %fusion.4, s32[1024]{0:T(1024)S(1)} %pad_clamp_fusion.3), kind=kCustom, calls=%fused_computation | custom fusion | bytes 3145824 | tf_op jit(solution)/shard_map/gather | solution.py:32
  29.4 34.1 %all-to-all-done = bf16[4,6,128,256]{3,2,1,0:T(8,128)(2,1)} async-done(((bf16[4,6,128,256]{3,2,1,0:T(8,128)(2,1)}), bf16[4,6,128,256]{3,2,1,0:T(8,128)(2,1)}, u32[]{:S(2)}, u32[]{:S(2)}) %all-to-all-start) | async-done | bytes 1572896 | tf_op jit(solution)/shard_map/all_to_all | solution.py:22
  63.5 3.3 %gather_fusion.2 = bf16[24,128,256]{2,1,0:T(8,128)(2,1)} fusion(bf16[24,128,256]{2,1,0:T(8,128)(2,1)} %bitcast.7, s32[1024]{0:T(1024)S(1)} %pad_clamp_fusion.1), kind=kCustom, calls=%fused_computation.2 | custom fusion | bytes 3145824 | tf_op jit(solution)/shard_map/gather | solution.py:27
  66.8 3.2 %multiply_convert_fusion = bf16[24,128,128]{2,1,0:T(8,128)(2,1)S(1)} fusion(s32[24,128,128]{2,1,0:T(8,128)} %param.8, bf16[24,128,256]{1,2,0:T(8,128)(2,1)} %gather_fusion, bf16[24,128,256]{2,1,0:T(8,128)(2,1)} %gather_fusion.2, f32[24]{0:T(128)S(1)} %compare_select_fusion.8), kind=kOutput, calls=%fused_computation.10 | convolution fusion | flops 202899456 | bytes 5505120 | tf_op jit(solution)/shard_map/ogj,omj->ogm/dot_general | solution.py:33
  70.0 1.8 %convolution_convert_fusion = bf16[24,128,256]{2,1,0:T(8,128)(2,1)} fusion(bf16[24,128,128]{2,1,0:T(8,128)(2,1)S(1)} %multiply_convert_fusion, bf16[24,128,256]{1,2,0:T(8,128)(2,1)S(1)} %copy-done.1), kind=kOutput, calls=%fused_computation.5 | convolution fusion | flops 202113024 | bytes 3932160 | tf_op jit(solution)/shard_map/yzj,yzh->yjh/dot_general | solution.py:47
  71.7 3.2 %gather_fusion.4 = bf16[24,128,256]{2,1,0:T(8,128)(2,1)} fusion(bf16[24,128,256]{2,1,0:T(8,128)(2,1)} %convolution_convert_fusion, s32[1024]{0:T(1024)S(1)} %pad_clamp_fusion), kind=kCustom, calls=%fused_computation.4 | custom fusion | bytes 3145824 | tf_op jit(solution)/shard_map/gather | solution.py:50
  75.0 4.5 %all-to-all-start.1 = ((bf16[4,6,128,256]{3,2,1,0:T(8,128)(2,1)}), bf16[4,6,128,256]{3,2,1,0:T(8,128)(2,1)}, u32[]{:S(2)}, u32[]{:S(2)}) async-start(bf16[4,6,128,256]{3,2,1,0:T(8,128)(2,1)} %bitcast.52), calls=%async_computation.1 | async-start | bytes 3145728 | tf_op jit(solution)/shard_map/all_to_all | solution.py:52
  79.5 0.0 reduce-scatter.2.cloned.1.call-start
  79.5 0.1 eq.19
  79.6 36.6 %all-to-all-done.1 = bf16[4,6,128,256]{3,2,1,0:T(8,128)(2,1)} async-done(((bf16[4,6,128,256]{3,2,1,0:T(8,128)(2,1)}), bf16[4,6,128,256]{3,2,1,0:T(8,128)(2,1)}, u32[]{:S(2)}, u32[]{:S(2)}) %all-to-all-start.1) | async-done | bytes 1572896 | tf_op jit(solution)/shard_map/all_to_all | solution.py:52
  116.2 2.6 %fusion = f32[8,128,256]{2,0,1:T(8,128)S(1)} fusion(s32[24]{0:T(128)S(1)} %eq.19, bf16[3,8,128,256]{3,2,1,0:T(8,128)(2,1)} %bitcast.19), kind=kOutput, calls=%fused_computation.7 | convolution fusion | flops 12583104 | bytes 2621536 | tf_op jit(solution)/shard_map/dot_general | solution.py:59
  118.8 1.3 copy.17
  120.2 0.0 reduce-scatter.2.cloned.1.call-update
  120.2 2.5 %gather_fusion.3 = bf16[24,256,256]{2,1,0:T(8,128)(2,1)} fusion(bf16[16,256,256]{2,1,0:T(8,128)(2,1)S(1)} %copy-done, s32[1024]{0:T(1024)S(1)} %pad_clamp_fusion.3), kind=kCustom, calls=%fused_computation.3 | custom fusion | bytes 6291552 | tf_op jit(solution)/shard_map/gather | solution.py:43
  122.7 31.8 %reduce-scatter.2.cloned.1.call-done = f32[1,128,256]{2,1,0:T(8,128)} async-done(((f32[8,128,256]{2,1,0:T(8,128)}), f32[1,128,256]{2,1,0:T(8,128)}) %reduce-scatter.2.cloned.1.call-update) | async-done | bytes 131088 | tf_op jit(solution)/shard_map/reduce_scatter | solution.py:65
  154.5 4.6 %fusion.6 = f32[128,256]{1,0:T(8,128)} fusion(bf16[24,256,256]{2,1,0:T(8,128)(2,1)} %gather_fusion.3, bf16[24,128,128]{2,1,0:T(8,128)(2,1)S(1)} %multiply_convert_fusion, bf16[24,128,256]{2,1,0:T(8,128)(2,1)} %gather_fusion.2, f32[1,128,256]{2,1,0:T(8,128)} %reduce-scatter.2.cloned.1.call-done), kind=kOutput, calls=%fused_computation.15 | convolution fusion | flops 604798976 | bytes 5767168 | tf_op jit(solution)/shard_map/tbs,trs->br/dot_general | solution.py:42
  (16 shorter events, 0.1 us)
Async XLA Ops:
  6.5 20.1 %copy-start = (bf16[16,256,256]{2,1,0:T(8,128)(2,1)S(1)}, bf16[16,256,256]{2,1,0:T(8,128)(2,1)}, u32[]{:S(2)}) copy-start(bf16[16,256,256]{2,1,0:T(8,128)(2,1)} %param.7) | copy-start | bytes 6291460
  20.9 5.7 %copy-start.4 = (s32[1,24]{1,0:T(1,128)S(1)}, s32[1,24]{1,0:T(1,128)}, u32[]{:S(2)}) copy-start(s32[1,24]{1,0:T(1,128)} %param.9) | copy-start | bytes 292
  20.9 5.7 %copy-start.2 = (bf16[128,256]{1,0:T(8,128)(2,1)S(1)}, bf16[128,256]{1,0:T(8,128)(2,1)}, u32[]{:S(2)}) copy-start(bf16[128,256]{1,0:T(8,128)(2,1)} %param.6) | copy-start | bytes 196612
  20.9 42.6 %all-to-all-start = ((bf16[4,6,128,256]{3,2,1,0:T(8,128)(2,1)}), bf16[4,6,128,256]{3,2,1,0:T(8,128)(2,1)}, u32[]{:S(2)}, u32[]{:S(2)}) async-start(bf16[4,6,128,256]{3,2,1,0:T(8,128)(2,1)} %bitcast.51), calls=%async_computation | async-start | bytes 3145728 | tf_op jit(solution)/shard_map/all_to_all | solution.py:22
  66.8 3.2 %copy-start.1 = (bf16[24,128,256]{1,2,0:T(8,128)(2,1)S(1)}, bf16[24,128,256]{1,2,0:T(8,128)(2,1)}, u32[]{:S(2)}) copy-start(bf16[24,128,256]{1,2,0:T(8,128)(2,1)} %gather_fusion) | copy-start | bytes 4718596
  75.0 4.5 %copy-start.3 = (s32[1,4,6]{2,1,0:T(4,128)S(1)}, s32[1,4,6]{2,1,0:T(4,128)}, u32[]{:S(2)}) copy-start(s32[1,4,6]{2,1,0:T(4,128)} %param.11) | copy-start | bytes 292
  75.0 41.2 %all-to-all-start.1 = ((bf16[4,6,128,256]{3,2,1,0:T(8,128)(2,1)}), bf16[4,6,128,256]{3,2,1,0:T(8,128)(2,1)}, u32[]{:S(2)}, u32[]{:S(2)}) async-start(bf16[4,6,128,256]{3,2,1,0:T(8,128)(2,1)} %bitcast.52), calls=%async_computation.1 | async-start | bytes 3145728 | tf_op jit(solution)/shard_map/all_to_all | solution.py:52
  79.5 75.0 %reduce-scatter.2.cloned.1.call-start = ((), (), s32[]{:S(2)}) async-start(), calls=%async_computation.3 | async-start | bytes 1179648 | tf_op jit(solution)/shard_map/reduce_scatter | solution.py:65
Sparse Core Ops, SparseCore 0:
  120.3 34.1 reduce-scatter.1
where the time goes:
time: 166 us
  waiting for transfers between devices  103 us (62%)
  local copies, waits for them, and re-layouts  15.2 us (9%)
  between operations  14.2 us (9%)
  matrix products  12.9 us (8%)
  blocking collectives  11.6 us (7%)
  starting transfers between devices  9.52 us (6%)
    all_to_all x1, waiting for transfers between devices, on_device(): lax.all_to_all(sent_terms, 'ent', split_axis=0, concat_axis=0, tiled=True)  36.6 us
    all_to_all x1, waiting for transfers between devices, on_device(): lax.all_to_all(outgoing, 'ent', split_axis=0, concat_axis=0, tiled=True)  34.1 us
    reduce_scatter x1, waiting for transfers between devices, on_device(): lax.psum_scatter(owner_terms.reshape(grp_count, block, width), 'grp', sca...  31.8 us
    all_gather x1, blocking collectives, on_device(): group_blocks = lax.all_gather(factor[None], 'grp', axis=0, tiled=True)  11.6 us
    all_to_all x1, starting transfers between devices, on_device(): lax.all_to_all(outgoing, 'ent', split_axis=0, concat_axis=0, tiled=True)  5 us
    dot_general x1, matrix products, on_device(): jnp.einsum('tbs,trs->br', relation_product, cores[relations], preferred_e...  4.58 us
    all_to_all x1, starting transfers between devices, on_device(): lax.all_to_all(sent_terms, 'ent', split_axis=0, concat_axis=0, tiled=True)  4.48 us
  transfers between devices with their start and end apart: 3, of which 3 were waited for; matrix products, arithmetic and copies ran while one was open for 3% of the time, Pallas kernels for 0%

commit v1 on v0

--- a/solution.py
+++ b/solution.py
@@ -4,6 +4,16 @@
 from jax.sharding import PartitionSpec as P
 
 LOSS_SCALE = 0.0625
+
+
+def pass_along(array, axis, dim):
+    devices = lax.axis_size(axis)
+    current, tiles = (array, [array])
+    for _ in range(devices - 1):
+        current = lax.ppermute(current, axis, [(i, (i + 1) % devices) for i in range(devices)])
+        tiles.insert(0, current)
+    line = jnp.concatenate(tiles, axis=dim)
+    return jnp.roll(line, (lax.axis_index(axis) + 1) * array.shape[dim], axis=dim)
 
 
 def on_device(factor, cores, adjacency, tile_rels, tile_count, send_lists):
@@ -17,7 +27,7 @@
     slots = ent_count * per_relay
     relations = tile_rels[0]
     routes = send_lists[0].reshape(slots)
-    group_blocks = lax.all_gather(factor[None], "grp", axis=0, tiled=True)
+    group_blocks = pass_along(factor[None], "grp", 0)
     outgoing = group_blocks[routes].reshape(ent_count, per_relay, block, width)
     arrived = lax.all_to_all(outgoing, "ent", split_axis=0, concat_axis=0, tiled=True).reshape(
         slots, block, width

time: 166 us -> 185 us (1.11)
  waiting for transfers between devices: 103 us -> 131 us
  blocking collectives: 11.6 us -> 0 us
    ppermute x0 -> x7, waiting for transfers between devices: none -> 31.8 us  [pass_along(): lax.ppermute(current, axis, [(i, (i + 1) % devices) for i in range(device...]
    all_gather x1 -> x0, blocking collectives: 11.6 us -> none  [on_device(): group_blocks = lax.all_gather(factor[None], 'grp', axis=0, tiled=True)]
    all_to_all x1, waiting for transfers between devices: 34.1 us -> 30.5 us  [on_device(): lax.all_to_all(outgoing, 'ent', split_axis=0, concat_axis=0, tiled=True)]
  transfers between devices with their start and end apart: 3 -> 10, of which waited for: 3 -> 10; matrix products, arithmetic and copies ran while one was open for 3% -> 3% of each run, Pallas kernels for 0% -> 0%
where the time goes in v1:
time: 185 us
  waiting for transfers between devices  131 us (71%)
  local copies, waits for them, and re-layouts  16 us (9%)
  between operations  14.3 us (8%)
  matrix products  12.9 us (7%)
  starting transfers between devices  10.7 us (6%)
    all_to_all x1, waiting for transfers between devices, on_device(): lax.all_to_all(sent_terms, 'ent', split_axis=0, concat_axis=0, tiled=True)  36.4 us
    reduce_scatter x1, waiting for transfers between devices, on_device(): lax.psum_scatter(owner_terms.reshape(grp_count, block, width), 'grp', sca...  32.3 us
    ppermute x7, waiting for transfers between devices, pass_along(): lax.ppermute(current, axis, [(i, (i + 1) % devices) for i in range(device...  31.8 us
    all_to_all x1, waiting for transfers between devices, on_device(): lax.all_to_all(outgoing, 'ent', split_axis=0, concat_axis=0, tiled=True)  30.5 us
    all_to_all x1, starting transfers between devices, on_device(): lax.all_to_all(outgoing, 'ent', split_axis=0, concat_axis=0, tiled=True)  5.73 us
    dot_general x1, matrix products, on_device(): jnp.einsum('tbs,trs->br', relation_product, cores[relations], preferred_e...  4.59 us
    all_to_all x1, starting transfers between devices, on_device(): lax.all_to_all(sent_terms, 'ent', split_axis=0, concat_axis=0, tiled=True)  4.49 us
  transfers between devices with their start and end apart: 10, of which 10 were waited for; matrix products, arithmetic and copies ran while one was open for 3% of the time, Pallas kernels for 0%

profile of v1, /device:TPU:0, one launch (start us, length us, event | category | flops | bytes accessed | tf_op | source)
XLA Modules:
  0.0 184.9 jit_solution(7478179014726687567)
XLA Ops:
  7.0 5.1 %collective-permute-done = bf16[1,128,256]{2,1,0:T(8,128)(2,1)S(1)} collective-permute-done((bf16[1,128,256]{2,1,0:T(8,128)(2,1)}, bf16[1,128,256]{2,1,0:T(8,128)(2,1)S(1)}, u32[]{:S(2)}, u32[]{:S(2)}) %collective-permute-start) | collective-permute-done | bytes 65568 | tf_op jit(solution)/shard_map/ppermute | solution.py:13
  12.1 4.6 %collective-permute-done.1 = bf16[1,128,256]{2,1,0:T(8,128)(2,1)S(1)} collective-permute-done((bf16[1,128,256]{2,1,0:T(8,128)(2,1)S(1)}, bf16[1,128,256]{2,1,0:T(8,128)(2,1)S(1)}, u32[]{:S(2)}, u32[]{:S(2)}) %collective-permute-start.1) | collective-permute-done | bytes 65568 | tf_op jit(solution)/shard_map/ppermute | solution.py:13
  16.7 4.6 %collective-permute-done.2 = bf16[1,128,256]{2,1,0:T(8,128)(2,1)S(1)} collective-permute-done((bf16[1,128,256]{2,1,0:T(8,128)(2,1)S(1)}, bf16[1,128,256]{2,1,0:T(8,128)(2,1)S(1)}, u32[]{:S(2)}, u32[]{:S(2)}) %collective-permute-start.2) | collective-permute-done | bytes 65568 | tf_op jit(solution)/shard_map/ppermute | solution.py:13
  21.2 0.8 reshape_squeeze.3
  22.0 3.8 %collective-permute-done.3 = bf16[1,128,256]{2,1,0:T(8,128)(2,1)S(1)} collective-permute-done((bf16[1,128,256]{2,1,0:T(8,128)(2,1)S(1)}, bf16[1,128,256]{2,1,0:T(8,128)(2,1)S(1)}, u32[]{:S(2)}, u32[]{:S(2)}) %collective-permute-start.3) | collective-permute-done | bytes 65568 | tf_op jit(solution)/shard_map/ppermute | solution.py:13
  25.8 4.6 %collective-permute-done.4 = bf16[1,128,256]{2,1,0:T(8,128)(2,1)S(1)} collective-permute-done((bf16[1,128,256]{2,1,0:T(8,128)(2,1)S(1)}, bf16[1,128,256]{2,1,0:T(8,128)(2,1)S(1)}, u32[]{:S(2)}, u32[]{:S(2)}) %collective-permute-start.4) | collective-permute-done | bytes 65568 | tf_op jit(solution)/shard_map/ppermute | solution.py:13
  30.5 4.6 %collective-permute-done.5 = bf16[1,128,256]{2,1,0:T(8,128)(2,1)S(1)} collective-permute-done((bf16[1,128,256]{2,1,0:T(8,128)(2,1)S(1)}, bf16[1,128,256]{2,1,0:T(8,128)(2,1)S(1)}, u32[]{:S(2)}, u32[]{:S(2)}) %collective-permute-start.5) | collective-permute-done | bytes 65568 | tf_op jit(solution)/shard_map/ppermute | solution.py:13
  35.0 4.6 %collective-permute-done.6 = bf16[1,128,256]{2,1,0:T(8,128)(2,1)S(1)} collective-permute-done((bf16[1,128,256]{2,1,0:T(8,128)(2,1)S(1)}, bf16[1,128,256]{2,1,0:T(8,128)(2,1)S(1)}, u32[]{:S(2)}, u32[]{:S(2)}) %collective-permute-start.6) | collective-permute-done | bytes 65568 | tf_op jit(solution)/shard_map/ppermute | solution.py:13
  39.7 0.8 constant_dynamic-update-slice_fusion.8
  40.7 1.9 %gather_fusion.1 = bf16[24,128,256]{2,1,0:T(8,128)(2,1)} fusion(bf16[8,128,256]{2,1,0:T(8,128)(2,1)S(1)} %constant_dynamic-slice_fusion, s32[1024]{0:T(1024)S(1)} %get-tuple-element.6), kind=kCustom, calls=%fused_computation.1 | custom fusion | bytes 3145824 | tf_op jit(solution)/shard_map/gather | solution.py:31
  42.6 5.7 %all-to-all-start = ((bf16[4,6,128,256]{3,2,1,0:T(8,128)(2,1)}), bf16[4,6,128,256]{3,2,1,0:T(8,128)(2,1)}, u32[]{:S(2)}, u32[]{:S(2)}) async-start(bf16[4,6,128,256]{3,2,1,0:T(8,128)(2,1)} %bitcast.52), calls=%async_computation | async-start | bytes 3145728 | tf_op jit(solution)/shard_map/all_to_all | solution.py:32
  49.8 1.9 %gather_fusion = bf16[24,128,256]{1,2,0:T(8,128)(2,1)} fusion(bf16[16,128,256]{1,2,0:T(8,128)(2,1)S(1)} %fusion.4, s32[1024]{0:T(1024)S(1)} %get-tuple-element.8), kind=kCustom, calls=%fused_computation | custom fusion | bytes 3145824 | tf_op jit(solution)/shard_map/gather | solution.py:42
  51.7 30.5 %all-to-all-done = bf16[4,6,128,256]{3,2,1,0:T(8,128)(2,1)} async-done(((bf16[4,6,128,256]{3,2,1,0:T(8,128)(2,1)}), bf16[4,6,128,256]{3,2,1,0:T(8,128)(2,1)}, u32[]{:S(2)}, u32[]{:S(2)}) %all-to-all-start) | async-done | bytes 1572896 | tf_op jit(solution)/shard_map/all_to_all | solution.py:32
  82.2 3.3 %gather_fusion.2 = bf16[24,128,256]{2,1,0:T(8,128)(2,1)} fusion(bf16[24,128,256]{2,1,0:T(8,128)(2,1)} %bitcast.7, s32[1024]{0:T(1024)S(1)} %get-tuple-element.7), kind=kCustom, calls=%fused_computation.2 | custom fusion | bytes 3145824 | tf_op jit(solution)/shard_map/gather | solution.py:37
  85.5 3.2 %multiply_convert_fusion = bf16[24,128,128]{2,1,0:T(8,128)(2,1)S(1)} fusion(s32[24,128,128]{2,1,0:T(8,128)} %param.8, bf16[24,128,256]{1,2,0:T(8,128)(2,1)} %gather_fusion, bf16[24,128,256]{2,1,0:T(8,128)(2,1)} %gather_fusion.2, f32[24]{0:T(128)S(1)} %compare_select_fusion.8), kind=kOutput, calls=%fused_computation.10 | convolution fusion | flops 202899456 | bytes 5505120 | tf_op jit(solution)/shard_map/ogj,omj->ogm/dot_general | solution.py:43
  88.6 1.8 convolution_convert_fusion
  90.4 3.3 %gather_fusion.4 = bf16[24,128,256]{2,1,0:T(8,128)(2,1)} fusion(bf16[24,128,256]{2,1,0:T(8,128)(2,1)} %convolution_convert_fusion, s32[1024]{0:T(1024)S(1)} %get-tuple-element.5), kind=kCustom, calls=%fused_computation.4 | custom fusion | bytes 3145824 | tf_op jit(solution)/shard_map/gather | solution.py:60
  93.7 4.5 %all-to-all-start.1 = ((bf16[4,6,128,256]{3,2,1,0:T(8,128)(2,1)}), bf16[4,6,128,256]{3,2,1,0:T(8,128)(2,1)}, u32[]{:S(2)}, u32[]{:S(2)}) async-start(bf16[4,6,128,256]{3,2,1,0:T(8,128)(2,1)} %bitcast.53), calls=%async_computation.1 | async-start | bytes 3145728 | tf_op jit(solution)/shard_map/all_to_all | solution.py:62
  98.3 36.4 %all-to-all-done.1 = bf16[4,6,128,256]{3,2,1,0:T(8,128)(2,1)} async-done(((bf16[4,6,128,256]{3,2,1,0:T(8,128)(2,1)}), bf16[4,6,128,256]{3,2,1,0:T(8,128)(2,1)}, u32[]{:S(2)}, u32[]{:S(2)}) %all-to-all-start.1) | async-done | bytes 1572896 | tf_op jit(solution)/shard_map/all_to_all | solution.py:62
  134.7 2.6 %fusion = f32[8,128,256]{2,0,1:T(8,128)S(1)} fusion(s32[24]{0:T(128)S(1)} %eq.22, bf16[3,8,128,256]{3,2,1,0:T(8,128)(2,1)} %bitcast.19), kind=kOutput, calls=%fused_computation.7 | convolution fusion | flops 12583104 | bytes 2621536 | tf_op jit(solution)/shard_map/dot_general | solution.py:69
  137.4 1.3 copy.17
  138.7 2.5 %gather_fusion.3 = bf16[24,256,256]{2,1,0:T(8,128)(2,1)} fusion(bf16[16,256,256]{2,1,0:T(8,128)(2,1)S(1)} %copy-done, s32[1024]{0:T(1024)S(1)} %get-tuple-element.8), kind=kCustom, calls=%fused_computation.3 | custom fusion | bytes 6291552 | tf_op jit(solution)/shard_map/gather | solution.py:53
  141.2 32.3 %reduce-scatter.2.cloned.1.call-done = f32[1,128,256]{2,1,0:T(8,128)} async-done(((f32[8,128,256]{2,1,0:T(8,128)}), f32[1,128,256]{2,1,0:T(8,128)}) %reduce-scatter.2.cloned.1.call-update) | async-done | bytes 131088 | tf_op jit(solution)/shard_map/reduce_scatter | solution.py:75
  173.5 4.6 %fusion.6 = f32[128,256]{1,0:T(8,128)} fusion(bf16[24,256,256]{2,1,0:T(8,128)(2,1)} %gather_fusion.3, bf16[24,128,128]{2,1,0:T(8,128)(2,1)S(1)} %multiply_convert_fusion, bf16[24,128,256]{2,1,0:T(8,128)(2,1)} %gather_fusion.2, f32[1,128,256]{2,1,0:T(8,128)} %reduce-scatter.2.cloned.1.call-done), kind=kOutput, calls=%fused_computation.15 | convolution fusion | flops 604798976 | bytes 5767168 | tf_op jit(solution)/shard_map/tbs,trs->br/dot_general | solution.py:52
  (44 shorter events, 1.6 us)
Async XLA Ops:
  6.5 42.5 %copy-start = (bf16[16,256,256]{2,1,0:T(8,128)(2,1)S(1)}, bf16[16,256,256]{2,1,0:T(8,128)(2,1)}, u32[]{:S(2)}) copy-start(bf16[16,256,256]{2,1,0:T(8,128)(2,1)} %param.7) | copy-start | bytes 6291460
  6.5 34.1 %copy-start.2 = (bf16[128,256]{1,0:T(8,128)(2,1)S(1)}, bf16[128,256]{1,0:T(8,128)(2,1)}, u32[]{:S(2)}) copy-start(bf16[128,256]{1,0:T(8,128)(2,1)} %param.6) | copy-start | bytes 196612
  6.5 5.5 %collective-permute-start = (bf16[1,128,256]{2,1,0:T(8,128)(2,1)}, bf16[1,128,256]{2,1,0:T(8,128)(2,1)S(1)}, u32[]{:S(2)}, u32[]{:S(2)}) collective-permute-start(bf16[1,128,256]{2,1,0:T(8,128)(2,1)} %bitcast.54), channel_id=1, source_target_pairs={{0,4},{4,8},{8,12},{12,16},{16,20},{20,24},{24,28},{28,0},{1,5},{5... | collective-permute-start | bytes 196616 | tf_op jit(solution)/shard_map/ppermute | solution.py:13
  12.1 4.6 %collective-permute-start.1 = (bf16[1,128,256]{2,1,0:T(8,128)(2,1)S(1)}, bf16[1,128,256]{2,1,0:T(8,128)(2,1)S(1)}, u32[]{:S(2)}, u32[]{:S(2)}) collective-permute-start(bf16[1,128,256]{2,1,0:T(8,128)(2,1)S(1)} %collective-permute-done), channel_id=1, source_target_pairs={{0,4},{4,8},{8,12},{12,16},{16,20},{20,24},{24,28},{28,0},{1,5},{5... | collective-permute-start | bytes 196616 | tf_op jit(solution)/shard_map/ppermute | solution.py:13
  16.7 4.6 %collective-permute-start.2 = (bf16[1,128,256]{2,1,0:T(8,128)(2,1)S(1)}, bf16[1,128,256]{2,1,0:T(8,128)(2,1)S(1)}, u32[]{:S(2)}, u32[]{:S(2)}) collective-permute-start(bf16[1,128,256]{2,1,0:T(8,128)(2,1)S(1)} %collective-permute-done.1), channel_id=1, source_target_pairs={{0,4},{4,8},{8,12},{12,16},{16,20},{20,24},{24,28},{28,0},{1,5},{5... | collective-permute-start | bytes 196616 | tf_op jit(solution)/shard_map/ppermute | solution.py:13
  21.2 4.6 %collective-permute-start.3 = (bf16[1,128,256]{2,1,0:T(8,128)(2,1)S(1)}, bf16[1,128,256]{2,1,0:T(8,128)(2,1)S(1)}, u32[]{:S(2)}, u32[]{:S(2)}) collective-permute-start(bf16[1,128,256]{2,1,0:T(8,128)(2,1)S(1)} %collective-permute-done.2), channel_id=1, source_target_pairs={{0,4},{4,8},{8,12},{12,16},{16,20},{20,24},{24,28},{28,0},{1,5},{5... | collective-permute-start | bytes 196616 | tf_op jit(solution)/shard_map/ppermute | solution.py:13
  25.8 4.6 %collective-permute-start.4 = (bf16[1,128,256]{2,1,0:T(8,128)(2,1)S(1)}, bf16[1,128,256]{2,1,0:T(8,128)(2,1)S(1)}, u32[]{:S(2)}, u32[]{:S(2)}) collective-permute-start(bf16[1,128,256]{2,1,0:T(8,128)(2,1)S(1)} %collective-permute-done.3), channel_id=1, source_target_pairs={{0,4},{4,8},{8,12},{12,16},{16,20},{20,24},{24,28},{28,0},{1,5},{5... | collective-permute-start | bytes 196616 | tf_op jit(solution)/shard_map/ppermute | solution.py:13
  30.4 4.6 %collective-permute-start.5 = (bf16[1,128,256]{2,1,0:T(8,128)(2,1)S(1)}, bf16[1,128,256]{2,1,0:T(8,128)(2,1)S(1)}, u32[]{:S(2)}, u32[]{:S(2)}) collective-permute-start(bf16[1,128,256]{2,1,0:T(8,128)(2,1)S(1)} %collective-permute-done.4), channel_id=1, source_target_pairs={{0,4},{4,8},{8,12},{12,16},{16,20},{20,24},{24,28},{28,0},{1,5},{5... | collective-permute-start | bytes 196616 | tf_op jit(solution)/shard_map/ppermute | solution.py:13
  35.0 4.6 %collective-permute-start.6 = (bf16[1,128,256]{2,1,0:T(8,128)(2,1)S(1)}, bf16[1,128,256]{2,1,0:T(8,128)(2,1)S(1)}, u32[]{:S(2)}, u32[]{:S(2)}) collective-permute-start(bf16[1,128,256]{2,1,0:T(8,128)(2,1)S(1)} %collective-permute-done.5), channel_id=1, source_target_pairs={{0,4},{4,8},{8,12},{12,16},{16,20},{20,24},{24,28},{28,0},{1,5},{5... | collective-permute-start | bytes 196616 | tf_op jit(solution)/shard_map/ppermute | solution.py:13
  42.6 6.4 %copy-start.4 = (s32[1,24]{1,0:T(1,128)S(1)}, s32[1,24]{1,0:T(1,128)}, u32[]{:S(2)}) copy-start(s32[1,24]{1,0:T(1,128)} %param.9) | copy-start | bytes 292
  42.6 39.6 %all-to-all-start = ((bf16[4,6,128,256]{3,2,1,0:T(8,128)(2,1)}), bf16[4,6,128,256]{3,2,1,0:T(8,128)(2,1)}, u32[]{:S(2)}, u32[]{:S(2)}) async-start(bf16[4,6,128,256]{3,2,1,0:T(8,128)(2,1)} %bitcast.52), calls=%async_computation | async-start | bytes 3145728 | tf_op jit(solution)/shard_map/all_to_all | solution.py:32
  85.5 3.2 %copy-start.1 = (bf16[24,128,256]{1,2,0:T(8,128)(2,1)S(1)}, bf16[24,128,256]{1,2,0:T(8,128)(2,1)}, u32[]{:S(2)}) copy-start(bf16[24,128,256]{1,2,0:T(8,128)(2,1)} %gather_fusion) | copy-start | bytes 4718596
  93.7 4.5 %copy-start.3 = (s32[1,4,6]{2,1,0:T(4,128)S(1)}, s32[1,4,6]{2,1,0:T(4,128)}, u32[]{:S(2)}) copy-start(s32[1,4,6]{2,1,0:T(4,128)} %param.11) | copy-start | bytes 292
  93.7 41.0 %all-to-all-start.1 = ((bf16[4,6,128,256]{3,2,1,0:T(8,128)(2,1)}), bf16[4,6,128,256]{3,2,1,0:T(8,128)(2,1)}, u32[]{:S(2)}, u32[]{:S(2)}) async-start(bf16[4,6,128,256]{3,2,1,0:T(8,128)(2,1)} %bitcast.53), calls=%async_computation.1 | async-start | bytes 3145728 | tf_op jit(solution)/shard_map/all_to_all | solution.py:62
  98.2 75.3 %reduce-scatter.2.cloned.1.call-start = ((), (), s32[]{:S(2)}) async-start(), calls=%async_computation.3 | async-start | bytes 1179648 | tf_op jit(solution)/shard_map/reduce_scatter | solution.py:75
Sparse Core Ops, SparseCore 0:
  138.8 34.6 reduce-scatter.1
